TPU v7x, 256 devices: a whole 4x4x8 slice. The times are simulated.
256 devices in a mesh: dp: 32 (over z, y), expert: 8 (over x, core).
Axes of the slice: x: 4, y: 4, z: 8, core: 2. Of those that a mesh axis runs over, the one named last changes fastest.
Arguments:
- residual: bfloat16 [2048, 4096], P(('dp', 'expert')), may hold values from -8.2 to 8.2
- queries: bfloat16 [2048, 4096], P('dp', 'expert'), may hold values from -24 to 24
- new_keys: bfloat16 [2048, 1024], P('dp', 'expert'), may hold values from -6 to 6
- new_values: bfloat16 [2048, 1024], P('dp', 'expert'), may hold values from -6 to 6
- cache_keys: bfloat16 [64, 1024, 1024], P('dp', None, 'expert'), may hold values from -8 to 8
- cache_values: bfloat16 [64, 1024, 1024], P('dp', None, 'expert'), may hold values from -6 to 6
- out_weight: bfloat16 [4096, 4096], P('expert', 'dp'), may hold values from -1 to 1
- ffn_gain: float32 [4096], replicated, may hold values from 0.1 to 1.9
- router: bfloat16 [4096, 8], replicated, may hold values from -0.0234375 to 0.0234375
- routes: int32 [2048, 2], P(('dp', 'expert')), may hold values from 0 to 7, all different within a row; in each aligned block of 64 rows (0 to 63, 64 to 127, ...) at most 24 rows name the same one
- w_gate: bfloat16 [8, 4096, 14336], P('expert', None, 'dp'), may hold values from -0.09375 to 0.09375
- w_up: bfloat16 [8, 4096, 14336], P('expert', None, 'dp'), may hold values from -0.09375 to 0.09375
- w_down: bfloat16 [8, 14336, 4096], P('expert', 'dp'), may hold values from -0.046875 to 0.046875
- summary_gain: float32 [4096], P('expert'), may hold values from 0.1 to 1.9
- reduce_scale: float32 [32], P('expert'), may hold values from 0.1 to 30
- assign: int32 [64], replicated, may hold values from 0 to 3
Outputs:
- summary: bfloat16 [64, 4096], P('dp', 'expert')
- reduced: bfloat16 [64, 4096], P('dp', 'expert')
Inputs may be any that keep to these rules, and one draw needn't show every extreme that they name: `routes`: each token names 2 different experts and every expert is named by some token; among the tokens of one dp index (aligned blocks of 64 rows) no expert is named by more than 24 tokens, and that bound is reached in some block.
All inputs are finite; a program needn't handle non-finite values.
Results may differ from a plain program's by a relative error of at most 0.017.
Values may be sent and summed in bfloat16 or wider, within the bound.
No kernel may reach another device: no remote copies, remote signals or barrier semaphores. Data moves between devices by JAX's collectives and lax.ppermute only.
A program may use at most 128 MiB of HBM per device.

v0:
```python
import math
import jax
import jax.numpy as jnp
from jax import lax
from jax.sharding import PartitionSpec as P

HEADS = 32
KVH = 8
HD = 128
EXPERTS = 8
WIN = 32
GROUP_CAP = 24
EPSILON = 1e-05


def attend(queries, new_keys, new_values, cache_keys, cache_values):
    span_count, cache_len, kv_width = cache_keys.shape
    kv_local = kv_width // HD
    group = HEADS // KVH
    window = queries.shape[0] // span_count
    query_view = queries.reshape(span_count, window, kv_local, group, HD)
    fresh_keys = new_keys.reshape(span_count, window, kv_local, HD)
    fresh_values = new_values.reshape(span_count, window, kv_local, HD)
    stored_keys = cache_keys.reshape(span_count, cache_len, kv_local, HD)
    stored_values = cache_values.reshape(span_count, cache_len, kv_local, HD)
    factor = 1.0 / math.sqrt(HD)
    past_scores = (
        jnp.einsum("ctkgd,cpkd->ckgtp", query_view, stored_keys, preferred_element_type=jnp.float32)
        * factor
    )
    fresh_scores = (
        jnp.einsum("ctkgd,cskd->ckgts", query_view, fresh_keys, preferred_element_type=jnp.float32)
        * factor
    )
    causal = jnp.arange(window)[:, None] >= jnp.arange(window)[None, :]
    fresh_scores = jnp.where(causal, fresh_scores, -jnp.inf)
    highest = jnp.maximum(jnp.max(past_scores, axis=-1), jnp.max(fresh_scores, axis=-1))[..., None]
    past_exp = jnp.exp(past_scores - highest)
    fresh_exp = jnp.exp(fresh_scores - highest)
    totals = jnp.sum(past_exp, axis=-1, keepdims=True) + jnp.sum(fresh_exp, axis=-1, keepdims=True)
    past_weights = (past_exp / totals).astype(jnp.bfloat16)
    fresh_weights = (fresh_exp / totals).astype(jnp.bfloat16)
    context = jnp.einsum(
        "ckgtp,cpkd->ctkgd", past_weights, stored_values, preferred_element_type=jnp.float32
    )
    context = context + jnp.einsum(
        "ckgts,cskd->ctkgd", fresh_weights, fresh_values, preferred_element_type=jnp.float32
    )
    return context.astype(jnp.bfloat16).reshape(span_count * window, kv_local * group * HD)


def expert_rows(rows, w_gate, w_up, w_down):
    gate_proj = jnp.einsum("ned,edf->nef", rows, w_gate, preferred_element_type=jnp.float32)
    up_proj = jnp.einsum("ned,edf->nef", rows, w_up, preferred_element_type=jnp.float32)
    hidden = (jax.nn.silu(gate_proj) * up_proj).astype(jnp.bfloat16)
    return jnp.einsum("nef,efd->ned", hidden, w_down, preferred_element_type=jnp.float32)


def shards(
    residual,
    queries,
    new_keys,
    new_values,
    cache_keys,
    cache_values,
    out_weight,
    ffn_gain,
    router,
    routes,
    w_gate,
    w_up,
    w_down,
    summary_gain,
    reduce_scale,
    assign,
):
    expert_count = lax.axis_size("expert")
    dp_index = lax.axis_index("dp")
    column = lax.axis_index("expert")
    span_local = cache_keys.shape[0]
    tok_local = residual.shape[0]
    width = residual.shape[1]
    slice_width = width // expert_count
    highest_precision = lax.Precision.HIGHEST
    attended = attend(queries, new_keys, new_values, cache_keys, cache_values)
    head_terms = jnp.dot(
        attended,
        lax.all_gather(out_weight, "dp", axis=1, tiled=True),
        preferred_element_type=jnp.float32,
    )
    mixed = residual.astype(jnp.float32) + lax.psum_scatter(
        head_terms, "expert", scatter_dimension=0, tiled=True
    )
    normed = (
        mixed * lax.rsqrt(jnp.mean(mixed * mixed, axis=-1, keepdims=True) + EPSILON) * ffn_gain
    ).astype(jnp.bfloat16)
    logits = jnp.dot(normed, router, preferred_element_type=jnp.float32)
    expert_ids = jnp.arange(EXPERTS, dtype=jnp.int32)
    first = routes[:, 0:1] == expert_ids[None, :]
    second = routes[:, 1:2] == expert_ids[None, :]
    first_logit = jnp.sum(jnp.where(first, logits, 0.0), axis=-1)
    second_logit = jnp.sum(jnp.where(second, logits, 0.0), axis=-1)
    partner = jnp.where(first, routes[:, 1:2], jnp.where(second, routes[:, 0:1], -1))
    outgoing = jnp.where((partner >= 0).T[:, :, None], normed[None, :, :], 0)
    arrived_rows, arrived_partner = (
        lax.all_to_all(outgoing, "expert", split_axis=0, concat_axis=1, tiled=True),
        lax.all_to_all(partner.T, "expert", split_axis=0, concat_axis=1, tiled=True),
    )
    present = (arrived_partner >= 0).astype(jnp.int32)
    position = jnp.cumsum(present, axis=1) - 1
    picker = (present[:, None, :] > 0) & (
        position[:, None, :] == jnp.arange(GROUP_CAP)[None, :, None]
    )
    compact = jnp.einsum(
        "eks,esd->ked",
        picker.astype(jnp.bfloat16),
        arrived_rows,
        preferred_element_type=jnp.float32,
    ).astype(jnp.bfloat16)
    token_span = (column * tok_local + jnp.arange(tok_local)) // WIN
    pool_matrix = (token_span[None, :] == jnp.arange(span_local)[:, None]).astype(jnp.float32)
    gathered = lax.all_gather(compact, "dp", axis=0, tiled=True)
    returned = lax.psum_scatter(
        expert_rows(gathered, w_gate, w_up, w_down), "dp", scatter_dimension=0, tiled=True
    )
    spread = jnp.einsum(
        "eks,ked->esd", picker.astype(jnp.float32), returned, precision=highest_precision
    )
    back = lax.all_to_all(spread, "expert", split_axis=1, concat_axis=0, tiled=True)
    gate_table = jnp.where(first, jax.nn.sigmoid(first_logit - second_logit)[:, None], 0.0)
    gate_table = gate_table + jnp.where(
        second, jax.nn.sigmoid(second_logit - first_logit)[:, None], 0.0
    )
    token_out = mixed + jnp.einsum("te,etd->td", gate_table, back, precision=highest_precision)
    pooled_local = jnp.dot(pool_matrix, token_out, precision=highest_precision)
    pooled = lax.psum_scatter(pooled_local, "expert", scatter_dimension=1, tiled=True)
    squares = lax.psum(jnp.sum(pooled * pooled, axis=-1), "expert")
    summary = (pooled * lax.rsqrt(squares / width + EPSILON)[:, None] * summary_gain).astype(
        jnp.bfloat16
    )
    everyone = lax.all_gather(summary, "dp", axis=0, tiled=True)
    heads_local = slice_width // HD
    mine = summary.reshape(span_local, heads_local, HD)
    others = everyone.reshape(everyone.shape[0], heads_local, HD)
    factor = reduce_scale / math.sqrt(HD)
    scores = (
        jnp.einsum("chd,khd->hck", mine, others, preferred_element_type=jnp.float32)
        * factor[:, None, None]
    )
    own_assign = lax.dynamic_slice_in_dim(assign, dp_index * span_local, span_local)
    same = own_assign[:, None] == assign[None, :]
    scores = jnp.where(same[None], scores, -jnp.inf)
    highest = jnp.max(scores, axis=-1, keepdims=True)
    expo = jnp.exp(scores - highest)
    weights = (expo / jnp.sum(expo, axis=-1, keepdims=True)).astype(jnp.bfloat16)
    reduced = jnp.einsum("hck,khd->chd", weights, others, preferred_element_type=jnp.float32)
    reduced = reduced.reshape(span_local, slice_width).astype(jnp.bfloat16)
    return (summary, reduced)


def solution(mesh):
    return jax.shard_map(
        shards,
        mesh=mesh,
        in_specs=(
            P(("dp", "expert"), None),
            P("dp", "expert"),
            P("dp", "expert"),
            P("dp", "expert"),
            P("dp", None, "expert"),
            P("dp", None, "expert"),
            P("expert", "dp"),
            P(),
            P(),
            P(("dp", "expert"), None),
            P("expert", None, "dp"),
            P("expert", None, "dp"),
            P("expert", "dp", None),
            P("expert"),
            P("expert"),
            P(),
        ),
        out_specs=(P("dp", "expert"), P("dp", "expert")),
        check_vma=False,
    )
```

profile of v0, /device:TPU:8, one launch (start us, length us, event | category | flops | bytes accessed | tf_op | source)
XLA Modules:
  0.0 635.6 jit_solution(1223442760722272505)
XLA Ops:
  7.2 0.7 all-gather.4.cloned.1.call-update
  8.0 0.9 reshape.508
  8.9 0.4 fusion.82
  9.2 1.0 fusion.83
  10.3 0.3 fusion.49
  10.6 0.9 fusion.61
  11.5 0.4 fusion.42
  12.0 84.5 %all-gather.4.cloned.1.call-done = bf16[512,4096]{1,0:T(8,128)(2,1)} async-done(((bf16[512,128]{1,0:T(8,128)(2,1)}), bf16[512,4096]{1,0:T(8,128)(2,1)}) %all-gather.4.cloned.1.call-update) | async-done | bytes 4194320 | tf_op jit(solution)/shard_map/all_gather | solution.py:88
  96.5 4.0 fusion.58
  100.5 0.6 compare_select_fusion.1
  101.1 4.3 all-to-all-start
  105.4 30.2 %reduce-scatter.6.cloned.1.call-done = f32[8,4096]{1,0:T(8,128)} async-done(((f32[64,4096]{1,0:T(8,128)}), f32[8,4096]{1,0:T(8,128)}) %reduce-scatter.6.cloned.1.call-update) | async-done | bytes 131088 | tf_op jit(solution)/shard_map/reduce_scatter | solution.py:91
  135.5 1.1 multiply_reduce_fusion
  136.6 1.0 multiply_convert_fusion
  137.6 0.9 broadcast_select_fusion
  138.5 3.5 all-to-all-start.1
  142.1 0.1 reshape.533
  142.2 0.1 gt.13
  142.3 0.1 reduce-window.7
  142.4 0.1 add_reduce_fusion
  142.5 9.8 %all-to-all-done.1 = bf16[8,8,4096]{2,1,0:T(8,128)(2,1)S(1)} async-done(((bf16[8,8,4096]{2,1,0:T(8,128)(2,1)}), bf16[8,8,4096]{2,1,0:T(8,128)(2,1)S(1)}, u32[]{:S(2)}, u32[]{:S(2)}) %all-to-all-start.1) | async-done | bytes 524320 | tf_op jit(solution)/shard_map/all_to_all | solution.py:106
  152.2 0.9 fusion.5
  153.1 0.2 reduce-scatter.8.cloned.1.call-start
  153.4 86.4 %all-gather.6.cloned.1.call-done = bf16[768,1,4096]{2,0,1:T(8,128)(2,1)} async-done(((bf16[24,1,4096]{2,0,1:T(8,128)(2,1)}), bf16[768,1,4096]{2,0,1:T(8,128)(2,1)}) %all-gather.6.cloned.1.call-update) | async-done | bytes 6291472 | tf_op jit(solution)/shard_map/all_gather | solution.py:122
  239.8 6.9 %fusion.9 = f32[768,1,448]{0,2,1:T(8,128)S(1)} fusion(bf16[1,4096,448]{1,2,0:T(8,128)(2,1)} %param.26, bf16[768,1,4096]{2,0,1:T(8,128)(2,1)} %all-gather.6.cloned.1.call-done), kind=kOutput, calls=%fused_computation.13 | convolution fusion | flops 2818572288 | bytes 11337728 | tf_op jit(solution)/shard_map/ned,edf->nef/dot_general | solution.py:53
  246.7 17.8 %convolution_bitcast_fusion = f32[768,1,4096]{2,0,1:T(8,128)} fusion(bf16[1,448,4096]{2,1,0:T(8,128)(2,1)} %param.28, bf16[1,4096,448]{1,2,0:T(8,128)(2,1)} %param.27, bf16[768,1,4096]{2,0,1:T(8,128)(2,1)} %all-gather.6.cloned.1.call-done, f32[768,1,448]{0,2,1:T(8,128)S(1)} %fusion.9), kind=kOutput, calls=%fused_computation.1 | convolution fusion | flops 5639208960 | bytes 27590656 | tf_op jit(solution)/shard_map/nef,efd->ned/dot_general | solution.py:56
  264.6 236.8 %reduce-scatter.8.cloned.1.call-done = f32[24,1,4096]{2,0,1:T(8,128)} async-done(((f32[768,1,4096]{2,0,1:T(8,128)}), f32[24,1,4096]{2,0,1:T(8,128)}) %reduce-scatter.8.cloned.1.call-update) | async-done | bytes 393232 | tf_op jit(solution)/shard_map/reduce_scatter | solution.py:123
  501.4 1.6 convolution_bitcast_fusion.2
  503.0 2.1 copy.45
  505.1 4.3 all-to-all-start.2
  509.3 0.3 reduce-scatter.10.cloned.1.call-start
  509.6 0.1 dynamic_slice.3
  509.7 0.2 select_reduce_fusion.1
  509.9 0.1 copy.54
  510.0 15.3 %all-to-all-done.2 = f32[1,64,4096]{2,0,1:T(1,128)S(1)} async-done(((f32[1,64,4096]{2,0,1:T(1,128)}), f32[1,64,4096]{2,0,1:T(1,128)S(1)}, u32[]{:S(2)}, u32[]{:S(2)}) %all-to-all-start.2) | async-done | bytes 1048608 | tf_op jit(solution)/shard_map/all_to_all | solution.py:129
  525.3 0.6 copy.86
  525.9 1.5 fusion.47
  527.4 3.2 convolution_bitcast_fusion.1
  530.6 0.1 broadcast_compare_fusion
  530.7 34.0 %reduce-scatter.10.cloned.1.call-done = f32[512,2]{1,0:T(8,128)} async-done(((f32[4096,2]{1,0:T(8,128)}), f32[512,2]{1,0:T(8,128)}) %reduce-scatter.10.cloned.1.call-update) | async-done | bytes 4112
  564.6 1.1 copy.58
  565.7 0.1 multiply_reduce_fusion.1
  565.8 12.9 %psum.7 = f32[2]{0:T(128)S(1)} all-reduce(f32[2]{0:T(128)S(1)} %multiply_reduce_fusion.1), channel_id=1, replica_groups=mesh['dp'=32,'expert'=8] {'expert'}, use_global_device_ids=true, to_apply=%region_12.13 | all-reduce | flops 2 | bytes 16 | tf_op jit(solution)/shard_map/psum | solution.py:137
  578.8 0.1 multiply_convert_fusion.1
  578.8 0.1 fusion.95
  578.9 49.0 %all-gather = bf16[32,2,512]{2,1,0:T(2,128)(2,1)S(1)} all-gather(bf16[1,2,512]{2,1,0:T(2,128)(2,1)S(1)} %fusion.95), channel_id=1, replica_groups=mesh['dp'=32,'expert'=8] {'dp'}, dimensions={0}, use_global_device_ids=true | all-gather | bytes 67584 | tf_op jit(solution)/shard_map/all_gather | solution.py:141
  628.0 0.3 fusion.84
  628.3 0.8 fusion.46
  (46 shorter events, 0.5 us)
Async XLA Ops:
  7.2 1.7 copy-start
  7.2 4.3 copy-start.8
  7.2 89.3 %all-gather.4.cloned.1.call-start = ((), (), s32[]{:S(2)}) async-start(), calls=%async_computation.6 | async-start | bytes 4325376 | tf_op jit(solution)/shard_map/all_gather | solution.py:88
  7.9 127.6 %reduce-scatter.6.cloned.1.call-start = ((), (), s32[]{:S(2)}) async-start(), calls=%async_computation.7 | async-start | bytes 1179648 | tf_op jit(solution)/shard_map/reduce_scatter | solution.py:91
  11.9 88.6 %copy-start.7 = (s32[8,2]{0,1:T(2,128)S(1)}, s32[8,2]{0,1:T(2,128)}, u32[]{:S(2)}) copy-start(s32[8,2]{0,1:T(2,128)} %param.25) | copy-start | bytes 196
  11.9 123.6 %copy-start.2 = (bf16[8,4096]{1,0:T(8,128)(2,1)S(1)}, bf16[8,4096]{1,0:T(8,128)(2,1)}, u32[]{:S(2)}) copy-start(bf16[8,4096]{1,0:T(8,128)(2,1)} %param.16) | copy-start | bytes 196612
  11.9 124.7 %copy-start.4 = (f32[4096]{0:T(1024)S(1)}, f32[4096]{0:T(1024)}, u32[]{:S(2)}) copy-start(f32[4096]{0:T(1024)} %param.23) | copy-start | bytes 49156
  101.1 37.4 %all-to-all-start = ((s32[8,1,8]{2,1,0:T(1,128)}), s32[8,1,8]{2,1,0:T(1,128)S(1)}, u32[]{:S(2)}, u32[]{:S(2)}) async-start(s32[8,1,8]{2,1,0:T(1,128)} %compare_select_fusion.1), calls=%async_computation.1 | async-start | bytes 8192 | tf_op jit(solution)/shard_map/all_to_all | solution.py:107
  138.5 13.7 %all-to-all-start.1 = ((bf16[8,8,4096]{2,1,0:T(8,128)(2,1)}), bf16[8,8,4096]{2,1,0:T(8,128)(2,1)S(1)}, u32[]{:S(2)}, u32[]{:S(2)}) async-start(bf16[8,8,4096]{2,1,0:T(8,128)(2,1)} %broadcast_select_fusion), calls=%async_computation.2 | async-start | bytes 1048576 | tf_op jit(solution)/shard_map/all_to_all | solution.py:106
  142.0 97.8 %all-gather.6.cloned.1.call-start = ((), (), s32[]{:S(2)}) async-start(), calls=%async_computation.8 | async-start | bytes 6488064 | tf_op jit(solution)/shard_map/all_gather | solution.py:122
  153.1 348.2 %reduce-scatter.8.cloned.1.call-start = ((), (), s32[]{:S(2)}) async-start(), calls=%async_computation.9 | async-start | bytes 12976128 | tf_op jit(solution)/shard_map/reduce_scatter | solution.py:123
  264.5 245.1 %copy-start.9 = (s32[64]{0:T(128)S(1)}, s32[64]{0:T(128)}, u32[]{:S(2)}) copy-start(s32[64]{0:T(128)} %param.31) | copy-start | bytes 772
  264.6 245.1 %copy-start.3 = (bf16[4096,8]{0,1:T(8,128)(2,1)S(1)}, bf16[4096,8]{0,1:T(8,128)(2,1)}, u32[]{:S(2)}) copy-start(bf16[4096,8]{0,1:T(8,128)(2,1)} %param.24) | copy-start | bytes 196612
  503.0 24.4 %copy-start.1 = (f32[8,4096]{1,0:T(8,128)S(1)}, f32[8,4096]{1,0:T(8,128)}, u32[]{:S(2)}) copy-start(f32[8,4096]{1,0:T(8,128)} %reduce-scatter.6.cloned.1.call-done) | copy-start | bytes 393220
  505.1 20.2 %all-to-all-start.2 = ((f32[1,64,4096]{2,0,1:T(1,128)}), f32[1,64,4096]{2,0,1:T(1,128)S(1)}, u32[]{:S(2)}, u32[]{:S(2)}) async-start(f32[1,64,4096]{2,0,1:T(1,128)} %copy.45), calls=%async_computation.4 | async-start | bytes 2097152 | tf_op jit(solution)/shard_map/all_to_all | solution.py:129
  509.3 55.3 %reduce-scatter.10.cloned.1.call-start = ((), (), s32[]{:S(2)}) async-start(), calls=%async_computation.10 | async-start | bytes 2359296
  510.0 55.9 %copy-start.10 = (f32[4]{0:T(128)S(1)}, f32[4]{0:T(128)}, u32[]{:S(2)}) copy-start(f32[4]{0:T(128)} %param.30) | copy-start | bytes 52
  510.0 68.8 %copy-start.5 = (f32[512]{0:T(512)S(1)}, f32[512]{0:T(512)}, u32[]{:S(2)}) copy-start(f32[512]{0:T(512)} %param.29) | copy-start | bytes 6148
  578.8 50.3 %copy-start.6 = (bf16[2,512]{1,0:T(2,128)(2,1)}, bf16[2,512]{1,0:T(2,128)(2,1)S(1)}, u32[]{:S(2)}) copy-start(bf16[2,512]{1,0:T(2,128)(2,1)S(1)} %multiply_convert_fusion.1) | copy-start | bytes 6148
Sparse Core Ops, SparseCore 0:
  10.5 85.9 all-gather.3
  100.6 34.8 reduce-scatter.5
  153.3 86.4 all-gather.5
  264.7 236.6 reduce-scatter.7
  530.7 33.8 reduce-scatter.9
where the time goes:
time: 636 us
  waiting for transfers between devices  498 us (78%)
  blocking collectives  61.9 us (10%)
  matrix products  39.8 us (6%)
  between operations  14.1 us (2%)
  starting transfers between devices  12.6 us (2%)
    reduce_scatter x1, waiting for transfers between devices, shards(): lax.psum_scatter(expert_rows(gathered, w_gate, w_up, w_down), 'dp', scatt...  237 us
    all_gather x1, waiting for transfers between devices, shards(): gathered = lax.all_gather(compact, 'dp', axis=0, tiled=True)  86.4 us
    all_gather x1, waiting for transfers between devices, shards(): lax.all_gather(out_weight, 'dp', axis=1, tiled=True)  84.5 us
    all_gather x1, blocking collectives, shards(): everyone = lax.all_gather(summary, 'dp', axis=0, tiled=True)  49 us
    unnamed x6, waiting for transfers between devices  34.7 us
    reduce_scatter x1, waiting for transfers between devices, shards(): lax.psum_scatter(head_terms, 'expert', scatter_dimension=0, tiled=True)  30.2 us
    dot_general x1, matrix products, expert_rows(): jnp.einsum('nef,efd->ned', hidden, w_down, preferred_element_type=jnp.flo...  17.8 us
    all_to_all x1, waiting for transfers between devices, shards(): lax.all_to_all(spread, 'expert', split_axis=1, concat_axis=0, tiled=True)  15.3 us
  transfers between devices with their start and end apart: 8, of which 7 were waited for; matrix products, arithmetic and copies ran while one was open for 1% of the time, Pallas kernels for 0%

commit v1 on v0

--- a/solution.py
+++ b/solution.py
@@ -119,7 +119,9 @@
     ).astype(jnp.bfloat16)
     token_span = (column * tok_local + jnp.arange(tok_local)) // WIN
     pool_matrix = (token_span[None, :] == jnp.arange(span_local)[:, None]).astype(jnp.float32)
-    gathered = lax.all_gather(compact, "dp", axis=0, tiled=True)
+    gathered = jnp.concatenate(
+        lax.all_to_all(jnp.stack([compact] * lax.axis_size("dp")), "dp", 0, 0), axis=0
+    )
     returned = lax.psum_scatter(
         expert_rows(gathered, w_gate, w_up, w_down), "dp", scatter_dimension=0, tiled=True
     )

time: 636 us -> 695 us (1.093)
  blocking collectives: 61.9 us -> 212 us
  waiting for transfers between devices: 498 us -> 408 us
    all_to_all x0 -> x1, blocking collectives: none -> 150 us  [shards(): lax.all_to_all(jnp.stack([compact] * lax.axis_size('dp')), 'dp', 0, 0)]
    all_gather x1 -> x0, waiting for transfers between devices: 86.4 us -> none  [shards(): gathered = lax.all_gather(compact, 'dp', axis=0, tiled=True)]
    unnamed x6 -> x5, waiting for transfers between devices: 34.7 us -> 34.7 us
  transfers between devices with their start and end apart: 8 -> 7, of which waited for: 7 -> 6; matrix products, arithmetic and copies ran while one was open for 1% -> 1% of each run, Pallas kernels for 0% -> 0%
where the time goes in v1:
time: 695 us
  waiting for transfers between devices  408 us (59%)
  blocking collectives  212 us (31%)
  matrix products  35.3 us (5%)
  between operations  14.1 us (2%)
  starting transfers between devices  12.4 us (2%)
  local copies, waits for them, and re-layouts  8.43 us (1%)
    reduce_scatter x1, waiting for transfers between devices, shards(): lax.psum_scatter(expert_rows(gathered, w_gate, w_up, w_down), 'dp', scatt...  233 us
    all_to_all x1, blocking collectives, shards(): lax.all_to_all(jnp.stack([compact] * lax.axis_size('dp')), 'dp', 0, 0)  150 us
    all_gather x1, waiting for transfers between devices, shards(): lax.all_gather(out_weight, 'dp', axis=1, tiled=True)  84.5 us
    all_gather x1, blocking collectives, shards(): everyone = lax.all_gather(summary, 'dp', axis=0, tiled=True)  49 us
    unnamed x5, waiting for transfers between devices  34.7 us
    reduce_scatter x1, waiting for transfers between devices, shards(): lax.psum_scatter(head_terms, 'expert', scatter_dimension=0, tiled=True)  30.2 us
    dot_general x1, matrix products, expert_rows(): jnp.einsum('nef,efd->ned', hidden, w_down, preferred_element_type=jnp.flo...  17.9 us
    all_to_all x1, waiting for transfers between devices, shards(): lax.all_to_all(spread, 'expert', split_axis=1, concat_axis=0, tiled=True)  15.3 us
  transfers between devices with their start and end apart: 7, of which 6 were waited for; matrix products, arithmetic and copies ran while one was open for 1% of the time, Pallas kernels for 0%

profile of v1, /device:TPU:8, one launch (start us, length us, event | category | flops | bytes accessed | tf_op | source)
XLA Modules:
  0.0 694.8 jit_solution(9949856112654765376)
XLA Ops:
  7.2 0.7 all-gather.3.cloned.1.call-update
  8.0 0.9 reshape.514
  8.9 0.4 fusion.68
  9.2 1.0 fusion.69
  10.3 0.3 fusion.35
  10.6 0.9 fusion.47
  11.5 0.4 fusion.28
  12.0 84.5 %all-gather.3.cloned.1.call-done = bf16[512,4096]{1,0:T(8,128)(2,1)} async-done(((bf16[512,128]{1,0:T(8,128)(2,1)}), bf16[512,4096]{1,0:T(8,128)(2,1)}) %all-gather.3.cloned.1.call-update) | async-done | bytes 4194320 | tf_op jit(solution)/shard_map/all_gather | solution.py:88
  96.5 4.0 fusion.44
  100.5 0.6 compare_select_fusion.1
  101.1 4.3 all-to-all-start
  105.4 30.2 %reduce-scatter.6.cloned.1.call-done = f32[8,4096]{1,0:T(8,128)} async-done(((f32[64,4096]{1,0:T(8,128)}), f32[8,4096]{1,0:T(8,128)}) %reduce-scatter.6.cloned.1.call-update) | async-done | bytes 131088 | tf_op jit(solution)/shard_map/reduce_scatter | solution.py:91
  135.5 1.1 multiply_reduce_fusion
  136.6 1.0 multiply_convert_fusion
  137.6 0.9 broadcast_select_fusion
  138.5 3.5 all-to-all-start.1
  142.1 0.1 reshape.539
  142.2 0.1 gt.13
  142.3 0.1 reduce-window.7
  142.4 0.1 add_reduce_fusion
  142.5 9.8 %all-to-all-done.1 = bf16[8,8,4096]{2,1,0:T(8,128)(2,1)S(1)} async-done(((bf16[8,8,4096]{2,1,0:T(8,128)(2,1)}), bf16[8,8,4096]{2,1,0:T(8,128)(2,1)S(1)}, u32[]{:S(2)}, u32[]{:S(2)}) %all-to-all-start.1) | async-done | bytes 524320 | tf_op jit(solution)/shard_map/all_to_all | solution.py:106
  152.2 0.2 fusion.1
  152.4 0.8 stack.2
  153.2 150.4 %all_to_all.36 = bf16[32,24,1,4096]{3,1,2,0:T(8,128)(2,1)S(1)} all-to-all(bf16[32,24,1,4096]{3,1,2,0:T(8,128)(2,1)S(1)} %stack.2), channel_id=1, replica_groups=mesh['dp'=32,'expert'=8] {'dp'}, dimensions={0} | all-to-all | bytes 12582912 | tf_op jit(solution)/shard_map/all_to_all | solution.py:123
  303.7 2.6 copy-done.1
  306.3 3.1 fusion.7
  309.3 17.9 %convolution_bitcast_fusion = f32[768,1,4096]{2,0,1:T(8,128)} fusion(bf16[1,448,4096]{2,1,0:T(8,128)(2,1)} %param.28, bf16[768,4096]{1,0:T(8,128)(2,1)} %bitcast.151, bf16[1,4096,448]{1,2,0:T(8,128)(2,1)} %param.27, f32[768,1,448]{0,2,1:T(8,128)S(1)} %fusion.7), kind=kOutput, calls=%fused_computation.1 | convolution fusion | flops 5639208960 | bytes 27590656 | tf_op jit(solution)/shard_map/nef,efd->ned/dot_general | solution.py:56
  327.2 233.3 %reduce-scatter.8.cloned.1.call-done = f32[24,1,4096]{2,0,1:T(8,128)} async-done(((f32[768,1,4096]{2,0,1:T(8,128)}), f32[24,1,4096]{2,0,1:T(8,128)}) %reduce-scatter.8.cloned.1.call-update) | async-done | bytes 393232 | tf_op jit(solution)/shard_map/reduce_scatter | solution.py:125
  560.5 1.6 convolution_bitcast_fusion.2
  562.1 2.1 copy.45
  564.2 4.3 all-to-all-start.3
  568.5 0.3 reduce-scatter.10.cloned.1.call-start
  568.8 0.1 dynamic_slice.3
  568.9 0.2 select_reduce_fusion.1
  569.1 15.3 %all-to-all-done.3 = f32[1,64,4096]{2,0,1:T(1,128)S(1)} async-done(((f32[1,64,4096]{2,0,1:T(1,128)}), f32[1,64,4096]{2,0,1:T(1,128)S(1)}, u32[]{:S(2)}, u32[]{:S(2)}) %all-to-all-start.3) | async-done | bytes 1048608 | tf_op jit(solution)/shard_map/all_to_all | solution.py:131
  584.4 0.6 copy.86
  585.0 1.5 fusion.33
  586.5 3.2 convolution_bitcast_fusion.1
  589.7 0.1 broadcast_compare_fusion
  589.8 34.0 %reduce-scatter.10.cloned.1.call-done = f32[512,2]{1,0:T(8,128)} async-done(((f32[4096,2]{1,0:T(8,128)}), f32[512,2]{1,0:T(8,128)}) %reduce-scatter.10.cloned.1.call-update) | async-done | bytes 4112
  623.8 1.1 copy.58
  624.9 0.1 multiply_reduce_fusion.1
  625.0 12.9 %psum.7 = f32[2]{0:T(128)S(1)} all-reduce(f32[2]{0:T(128)S(1)} %multiply_reduce_fusion.1), channel_id=1, replica_groups=mesh['dp'=32,'expert'=8] {'expert'}, use_global_device_ids=true, to_apply=%region_12.13 | all-reduce | flops 2 | bytes 16 | tf_op jit(solution)/shard_map/psum | solution.py:139
  638.0 0.1 multiply_convert_fusion.1
  638.0 0.1 fusion.83
  638.1 49.0 %all-gather = bf16[32,2,512]{2,1,0:T(2,128)(2,1)S(1)} all-gather(bf16[1,2,512]{2,1,0:T(2,128)(2,1)S(1)} %fusion.83), channel_id=1, replica_groups=mesh['dp'=32,'expert'=8] {'dp'}, dimensions={0}, use_global_device_ids=true | all-gather | bytes 67584 | tf_op jit(solution)/shard_map/all_gather | solution.py:143
  687.2 0.3 fusion.70
  687.5 0.8 fusion.32
  (49 shorter events, 0.6 us)
Async XLA Ops:
  7.2 1.7 copy-start
  7.2 4.3 copy-start.10
  7.2 89.3 %all-gather.3.cloned.1.call-start = ((), (), s32[]{:S(2)}) async-start(), calls=%async_computation.7 | async-start | bytes 4325376 | tf_op jit(solution)/shard_map/all_gather | solution.py:88
  7.9 127.6 %reduce-scatter.6.cloned.1.call-start = ((), (), s32[]{:S(2)}) async-start(), calls=%async_computation.8 | async-start | bytes 1179648 | tf_op jit(solution)/shard_map/reduce_scatter | solution.py:91
  11.9 88.6 %copy-start.8 = (s32[8,2]{0,1:T(2,128)S(1)}, s32[8,2]{0,1:T(2,128)}, u32[]{:S(2)}) copy-start(s32[8,2]{0,1:T(2,128)} %param.25) | copy-start | bytes 196
  11.9 123.6 %copy-start.3 = (bf16[8,4096]{1,0:T(8,128)(2,1)S(1)}, bf16[8,4096]{1,0:T(8,128)(2,1)}, u32[]{:S(2)}) copy-start(bf16[8,4096]{1,0:T(8,128)(2,1)} %param.16) | copy-start | bytes 196612
  11.9 124.7 %copy-start.5 = (f32[4096]{0:T(1024)S(1)}, f32[4096]{0:T(1024)}, u32[]{:S(2)}) copy-start(f32[4096]{0:T(1024)} %param.23) | copy-start | bytes 49156
  101.1 37.4 %all-to-all-start = ((s32[8,1,8]{2,1,0:T(1,128)}), s32[8,1,8]{2,1,0:T(1,128)S(1)}, u32[]{:S(2)}, u32[]{:S(2)}) async-start(s32[8,1,8]{2,1,0:T(1,128)} %compare_select_fusion.1), calls=%async_computation.1 | async-start | bytes 8192 | tf_op jit(solution)/shard_map/all_to_all | solution.py:107
  138.5 13.7 %all-to-all-start.1 = ((bf16[8,8,4096]{2,1,0:T(8,128)(2,1)}), bf16[8,8,4096]{2,1,0:T(8,128)(2,1)S(1)}, u32[]{:S(2)}, u32[]{:S(2)}) async-start(bf16[8,8,4096]{2,1,0:T(8,128)(2,1)} %broadcast_select_fusion), calls=%async_computation.2 | async-start | bytes 1048576 | tf_op jit(solution)/shard_map/all_to_all | solution.py:106
  142.0 418.5 %reduce-scatter.8.cloned.1.call-start = ((), (), s32[]{:S(2)}) async-start(), calls=%async_computation.9 | async-start | bytes 12976128 | tf_op jit(solution)/shard_map/reduce_scatter | solution.py:125
  153.2 153.0 %copy-start.9 = (bf16[1,4096,448]{1,2,0:T(8,128)(2,1)S(1)}, bf16[1,4096,448]{1,2,0:T(8,128)(2,1)}, u32[]{:S(2)}) copy-start(bf16[1,4096,448]{1,2,0:T(8,128)(2,1)} %param.26) | copy-start | bytes 11010052
  303.7 2.6 copy-start.1
  327.2 241.5 %copy-start.11 = (s32[64]{0:T(128)S(1)}, s32[64]{0:T(128)}, u32[]{:S(2)}) copy-start(s32[64]{0:T(128)} %param.31) | copy-start | bytes 772
  327.2 241.6 %copy-start.4 = (bf16[4096,8]{0,1:T(8,128)(2,1)S(1)}, bf16[4096,8]{0,1:T(8,128)(2,1)}, u32[]{:S(2)}) copy-start(bf16[4096,8]{0,1:T(8,128)(2,1)} %param.24) | copy-start | bytes 196612
  562.1 24.4 %copy-start.2 = (f32[8,4096]{1,0:T(8,128)S(1)}, f32[8,4096]{1,0:T(8,128)}, u32[]{:S(2)}) copy-start(f32[8,4096]{1,0:T(8,128)} %reduce-scatter.6.cloned.1.call-done) | copy-start | bytes 393220
  564.2 20.2 %all-to-all-start.3 = ((f32[1,64,4096]{2,0,1:T(1,128)}), f32[1,64,4096]{2,0,1:T(1,128)S(1)}, u32[]{:S(2)}, u32[]{:S(2)}) async-start(f32[1,64,4096]{2,0,1:T(1,128)} %copy.45), calls=%async_computation.5 | async-start | bytes 2097152 | tf_op jit(solution)/shard_map/all_to_all | solution.py:131
  568.5 55.3 %reduce-scatter.10.cloned.1.call-start = ((), (), s32[]{:S(2)}) async-start(), calls=%async_computation.10 | async-start | bytes 2359296
  569.1 55.9 %copy-start.12 = (f32[4]{0:T(128)S(1)}, f32[4]{0:T(128)}, u32[]{:S(2)}) copy-start(f32[4]{0:T(128)} %param.30) | copy-start | bytes 52
  569.1 68.8 %copy-start.6 = (f32[512]{0:T(512)S(1)}, f32[512]{0:T(512)}, u32[]{:S(2)}) copy-start(f32[512]{0:T(512)} %param.29) | copy-start | bytes 6148
  638.0 50.3 %copy-start.7 = (bf16[2,512]{1,0:T(2,128)(2,1)}, bf16[2,512]{1,0:T(2,128)(2,1)S(1)}, u32[]{:S(2)}) copy-start(bf16[2,512]{1,0:T(2,128)(2,1)S(1)} %multiply_convert_fusion.1) | copy-start | bytes 6148
Sparse Core Ops, SparseCore 0:
  10.5 85.9 all-gather.2
  100.6 34.8 reduce-scatter.5
  327.3 233.1 reduce-scatter.7
  589.9 33.9 reduce-scatter.9
